TPU v7x, 512 devices: a whole 4x8x8 slice. The times are simulated.
512 devices in a mesh: shard: 128 (over y, z, core), tensor: 4 (over x).
Axes of the slice: x: 4, y: 8, z: 8, core: 2. Of those that a mesh axis runs over, the one named last changes fastest.
Arguments:
- big_grad: bfloat16 [32, 1280, 768], P(None, 'shard', 'tensor')
- big_weight: bfloat16 [32, 1280, 768], P(None, 'shard', 'tensor'), may hold values from -0.017944336 to 0.017944336
- big_moment: float32 [128, 768, 1280], P('shard', 'tensor'), may hold values from -6 to 6
- small_grad: bfloat16 [32, 1280, 192], P(None, 'shard')
- small_weight: bfloat16 [32, 1280, 192], P(None, 'shard'), may hold values from -0.15625 to 0.15625
- small_moment: float32 [128, 192, 1280], P('shard'), may hold values from -6 to 6
- owners: int32 [2, 32], replicated, may hold values from 0 to 127, as said below
- vec_parts: float32 [128, 43008], P('shard'), may hold values from -0.6 to 0.6
- vec_param: float32 [43008], P('shard'), may hold values from 0.5 to 1.5
- vec_first: float32 [43008], P('shard'), may hold values from -0.6 to 0.6
- vec_second: float32 [43008], P('shard'), may hold values from 0.01 to 1
Outputs:
- big_weight_new: bfloat16 [32, 1280, 768], P(None, 'shard', 'tensor')
- big_moment_new: float32 [128, 768, 1280], P('shard', 'tensor')
- small_weight_new: bfloat16 [32, 1280, 192], P(None, 'shard')
- small_moment_new: float32 [128, 192, 1280], P('shard')
- vec_param_new: float32 [43008], P('shard')
- vec_first_new: float32 [43008], P('shard')
- vec_second_new: float32 [43008], P('shard')
Inputs may be any that keep to these rules, and one draw needn't show every extreme that they name: `owners`: no shard index appears twice in the whole list (over both rows); each aligned group of four shard indices holds exactly one owner of each row; the first and the last shard index own a matrix.
All inputs are finite; a program needn't handle non-finite values.
Results may differ from a plain program's by a relative error of at most 0.0068.
Values may be sent and summed in bfloat16 or wider, within the bound.
No kernel may reach another device: no remote copies, remote signals or barrier semaphores. Data moves between devices by JAX's collectives and lax.ppermute only.
A program may use at most 64 MiB of HBM per device.

v0:
```python
import math
import jax
import jax.numpy as jnp
from jax import lax
from jax.sharding import PartitionSpec as P

D = 1280
ITERS = 2
newton_linear = 3.4445
newton_cubic = -4.775
newton_quintic = 2.0315
momentum_rate = 0.95
muon_rate = 0.05
weight_decay = 0.1
norm_epsilon = 1e-07
adam_rate = 0.004
first_decay = 0.9
second_decay = 0.95
adam_epsilon = 1e-08
first_correct = 0.99997343860111
second_correct = 0.99407947077967


def owner_table(owner_list, count):
    devices = lax.broadcasted_iota(jnp.int32, (count, owner_list.shape[0]), 0)
    return (devices == owner_list[None, :]).astype(jnp.bfloat16)


def route_rows(owner_map, pieces):
    flattened = pieces.reshape(pieces.shape[0], -1)
    routed = jnp.dot(owner_map, flattened, preferred_element_type=jnp.float32)
    return routed.astype(jnp.bfloat16).reshape((owner_map.shape[0],) + pieces.shape[1:])


def collect(owner_map, arrived):
    flattened = arrived.reshape(arrived.shape[0], -1)
    picked = lax.dot_general(
        owner_map, flattened, (((0,), (0,)), ((), ())), preferred_element_type=jnp.float32
    )
    return picked.astype(jnp.bfloat16).reshape((owner_map.shape[1],) + arrived.shape[1:])


def advance(arrived, moment, is_owner):
    gradient = arrived.T.astype(jnp.float32)
    renewed = momentum_rate * moment + gradient
    retained = jnp.where(is_owner, renewed, moment)
    blended = jnp.where(is_owner, gradient + momentum_rate * renewed, 0.0).astype(jnp.bfloat16).T
    return (retained, blended)


def normalized(field):
    values = field.astype(jnp.float32)
    squares = jnp.sum(values * values)
    return (values / (jnp.sqrt(squares) + norm_epsilon)).astype(jnp.bfloat16)


def gram_block(left_part, right_part):
    product = lax.dot_general(
        left_part, right_part, (((0,), (0,)), ((), ())), preferred_element_type=jnp.float32
    )
    return product.astype(jnp.bfloat16)


def poly_block(gram_part, gram_full):
    square = jnp.dot(gram_part, gram_full, preferred_element_type=jnp.float32)
    return (newton_cubic * gram_part.astype(jnp.float32) + newton_quintic * square).astype(
        jnp.bfloat16
    )


def newton_step(column_part, full_iterate, polynomial):
    product = lax.dot_general(
        full_iterate, polynomial, (((1,), (1,)), ((), ())), preferred_element_type=jnp.float32
    )
    return (newton_linear * column_part.astype(jnp.float32) + product).astype(jnp.bfloat16)


def small_newton(field):
    iterate = normalized(field)
    for iteration in range(ITERS):
        gram_full = gram_block(iterate, iterate)
        iterate = newton_step(iterate, iterate, poly_block(gram_full, gram_full))
    return iterate


def apply_update(weight, update):
    scale = 0.2 * math.sqrt(D)
    values = weight.astype(jnp.float32)
    return (
        values - muon_rate * (scale * update.astype(jnp.float32) + weight_decay * values)
    ).astype(jnp.bfloat16)


def gather_columns(column_part):
    return lax.all_gather(column_part, "tensor", axis=1, tiled=True)


def gather_gram(gram_part):
    return lax.all_gather(gram_part, "tensor", axis=0, tiled=True)


def per_device(
    big_grad,
    big_weight,
    big_moment,
    small_grad,
    small_weight,
    small_moment,
    owners,
    vec_parts,
    vec_param,
    vec_first,
    vec_second,
):
    shards = lax.axis_size("shard")
    shard_place = lax.axis_index("shard")
    column = lax.axis_index("tensor")
    block_width = big_grad.shape[2]
    rows_dev = big_grad.shape[1]
    matrices = big_grad.shape[0]
    joint_map = owner_table(jnp.concatenate([owners[0], owners[1]]), shards)
    joint_pieces = jnp.concatenate([big_grad, small_grad], axis=0)
    arrived = lax.all_to_all(
        route_rows(joint_map, joint_pieces), "shard", split_axis=0, concat_axis=1, tiled=True
    )[0]
    big_owner = jnp.any(owners[0] == shard_place)
    small_owner = jnp.any(owners[1] == shard_place)
    big_retained, big_blended = advance(arrived, big_moment[0], big_owner)
    small_retained, small_blended = advance(arrived, small_moment[0], small_owner)
    small_result = small_newton(small_blended)
    full_iterate = normalized(gather_columns(big_blended))
    for iteration in range(ITERS - 1):
        gram_full = gram_block(full_iterate, full_iterate)
        full_iterate = newton_step(full_iterate, full_iterate, poly_block(gram_full, gram_full))
    gram_full = gram_block(full_iterate, full_iterate)
    gram_rows = lax.dynamic_slice_in_dim(gram_full, column * block_width, block_width, 0)
    owned_part = lax.dynamic_slice_in_dim(full_iterate, column * block_width, block_width, 1)
    big_result = newton_step(owned_part, full_iterate, poly_block(gram_rows, gram_full))
    own_result = jnp.where(big_owner, big_result, small_result)
    returned = lax.all_to_all(
        own_result.reshape(shards, rows_dev, block_width),
        "shard",
        split_axis=0,
        concat_axis=0,
        tiled=True,
    )
    picked = collect(joint_map, returned)
    big_weight_new = apply_update(big_weight, picked[:matrices])
    small_weight_new = apply_update(small_weight, picked[matrices:])
    vec_pieces = vec_parts[0].reshape(shards, -1)
    grad_share = jnp.sum(
        lax.all_to_all(vec_pieces, "shard", split_axis=0, concat_axis=0, tiled=True), axis=0
    )
    first_new = first_decay * vec_first + (1.0 - first_decay) * grad_share
    second_new = second_decay * vec_second + (1.0 - second_decay) * grad_share * grad_share
    param_new = vec_param - adam_rate * (first_new / first_correct) / (
        jnp.sqrt(second_new / second_correct) + adam_epsilon
    )
    return (
        big_weight_new,
        big_retained[None],
        small_weight_new,
        small_retained[None],
        param_new,
        first_new,
        second_new,
    )


def solution(mesh):
    return jax.shard_map(
        per_device,
        mesh=mesh,
        in_specs=(
            P(None, "shard", "tensor"),
            P(None, "shard", "tensor"),
            P("shard", "tensor", None),
            P(None, "shard", None),
            P(None, "shard", None),
            P("shard", None, None),
            P(),
            P("shard", None),
            P("shard"),
            P("shard"),
            P("shard"),
        ),
        out_specs=(
            P(None, "shard", "tensor"),
            P("shard", "tensor", None),
            P(None, "shard", None),
            P("shard", None, None),
            P("shard"),
            P("shard"),
            P("shard"),
        ),
        check_vma=False,
    )
```

profile of v0, /device:TPU:1, one launch (start us, length us, event | category | flops | bytes accessed | tf_op | source)
XLA Modules:
  0.0 153.9 jit_solution(12986507688042528019)
XLA Ops:
  7.2 0.8 slice_bitcast_fusion.1
  7.9 1.0 pad_maximum_fusion
  9.0 0.2 copy.32
  9.2 0.4 reshape.45
  9.6 0.1 pad_add_fusion
  9.6 0.3 convolution_convert_fusion
  9.9 0.3 copy.33
  10.2 1.3 copy.34
  11.5 1.6 %reshape.59 = bf16[128,2,960]{2,1,0:T(2,128)(2,1)} reshape(bf16[128,10,192]{2,1,0:T(8,128)(2,1)S(1)} %copy.34) | data formatting | bytes 983040
  13.1 18.4 %all-to-all-start = ((bf16[128,2,960]{2,1,0:T(2,128)(2,1)}), bf16[128,2,960]{2,1,0:T(2,128)(2,1)S(1)}, u32[]{:S(2)}, u32[]{:S(2)}) async-start(bf16[128,2,960]{2,1,0:T(2,128)(2,1)} %reshape.59), calls=%async_computation | async-start | bytes 1048576 | tf_op jit(solution)/shard_map/all_to_all | solution.py:123
  31.5 0.0 all-gather.2.cloned.1.call-start
  31.6 0.6 compare_reduce_fusion.1
  32.2 18.7 %all-to-all-done = bf16[128,2,960]{2,1,0:T(2,128)(2,1)S(1)} async-done(((bf16[128,2,960]{2,1,0:T(2,128)(2,1)}), bf16[128,2,960]{2,1,0:T(2,128)(2,1)S(1)}, u32[]{:S(2)}, u32[]{:S(2)}) %all-to-all-start) | async-done | bytes 491552 | tf_op jit(solution)/shard_map/all_to_all | solution.py:123
  50.9 0.8 reshape.60
  51.7 0.4 reshape.49
  52.1 0.4 copy.35
  52.5 0.8 copy-done.1
  53.3 4.9 %fusion.17 = (f32[1,192,1280]{2,1,0:T(8,128)}, bf16[1280,192]{0,1:T(8,128)(2,1)}, f32[1,192,1280]{2,1,0:T(8,128)}, f32[]{:T(128)}, bf16[192,1280]{1,0:T(8,128)(2,1)S(1)}) fusion(f32[1,192,1280]{2,1,0:T(8,128)S(1)} %copy-done.1, f32[1280,192]{0,1:T(8,128)S(1)} %copy.35, pred[]{:T(512)} %get-tuple-element.21, f32[1,192,1280]{2,1,0:T(8,128)} %param.16, ...), kind=kLoop, calls=%fused_computation.39 | loop fusion | flops 4177919 | bytes 5898246 | tf_op jit(solution)/shard_map/broadcast_in_dim | solution.py:161
  58.2 0.5 broadcast.71
  58.7 1.0 reduce.5
  59.8 1.0 all_to_all.20
  60.8 7.3 %all-to-all-start.2 = ((f32[128,1,336]{2,1,0:T(1,128)}), f32[128,1,336]{2,1,0:T(1,128)S(1)}, u32[]{:S(2)}, u32[]{:S(2)}) async-start(f32[128,1,336]{2,1,0:T(1,128)} %all_to_all.20), calls=%async_computation.2 | async-start | bytes 393216 | tf_op jit(solution)/shard_map/all_to_all | solution.py:152
  68.7 0.3 convolution_convert_fusion.5
  69.1 0.4 fusion.3
  69.5 0.3 convolution_convert_fusion.4
  69.8 0.4 fusion.4
  70.3 16.5 %all-gather.2.cloned.1.call-done = bf16[1280,768]{0,1:T(8,128)(2,1)} async-done(((bf16[1280,192]{0,1:T(8,128)(2,1)}), bf16[1280,768]{0,1:T(8,128)(2,1)}) %all-gather.2.cloned.1.call-update) | async-done | bytes 1966096 | tf_op jit(solution)/shard_map/all_gather | solution.py:95
  86.8 3.3 %fusion = f32[]{:T(128)} fusion(bf16[1280,768]{0,1:T(8,128)(2,1)} %all-gather.2.cloned.1.call-done), kind=kLoop, calls=%fused_computation.2 | loop fusion | flops 2949119 | bytes 1966084 | tf_op jit(solution)/shard_map/reduce_sum | solution.py:53
  90.8 2.8 %convolution_convert_fusion.3 = bf16[768,768]{1,0:T(8,128)(2,1)} fusion(bf16[1280,768]{0,1:T(8,128)(2,1)S(1)} %copy-done, f32[]{:T(128)S(6)} %add.66), kind=kOutput, calls=%fused_computation.16 | convolution fusion | flops 1513488384 | bytes 3145732 | tf_op jit(solution)/shard_map/dot_general | solution.py:58
  93.6 6.3 %add_convert_fusion = bf16[1280,768]{0,1:T(8,128)(2,1)} fusion(bf16[768,768]{1,0:T(8,128)(2,1)} %convolution_convert_fusion.3, f32[]{:T(128)S(6)} %add.66, bf16[1280,768]{0,1:T(8,128)(2,1)S(1)} %copy-done), kind=kOutput, calls=%fused_computation.4 | convolution fusion | flops 2428698624 | bytes 5111812 | tf_op jit(solution)/shard_map/dot_general | solution.py:72
  99.9 3.8 %convolution_convert_fusion.2 = bf16[768,768]{1,0:T(8,128)(2,1)S(1)} fusion(bf16[1280,768]{0,1:T(8,128)(2,1)} %add_convert_fusion), kind=kOutput, calls=%fused_computation.15 | convolution fusion | flops 1510539264 | bytes 3145728 | tf_op jit(solution)/shard_map/dot_general | solution.py:58
  103.7 3.2 %fusion.5 = bf16[1280,192]{0,1:T(8,128)(2,1)S(1)} fusion(bf16[1280,192]{0,1:T(8,128)(2,1)S(1)} %fusion.4, bf16[1280,768]{0,1:T(8,128)(2,1)} %add_convert_fusion, bf16[768,768]{1,0:T(8,128)(2,1)S(1)} %convolution_convert_fusion.2, s32[]{:T(128)S(6)} %select_n.39, pred[]{:T(512)} %get-tuple-element.21), kind=kOutput, calls=%fused_computation.11 | convolution fusion | flops 605945856 | bytes 5212160 | tf_op jit(solution)/shard_map/dot_general | solution.py:72
  106.9 0.2 copy.36
  107.2 0.3 reshape.47
  107.5 1.6 %reshape.61 = bf16[128,2,960]{2,1,0:T(2,128)(2,1)} reshape(bf16[128,10,192]{2,1,0:T(8,128)(2,1)S(1)} %reshape.47) | data formatting | bytes 983040
  109.1 14.5 %all-to-all-start.1 = ((bf16[128,2,960]{2,1,0:T(2,128)(2,1)}), bf16[128,2,960]{2,1,0:T(2,128)(2,1)S(1)}, u32[]{:S(2)}, u32[]{:S(2)}) async-start(bf16[128,2,960]{2,1,0:T(2,128)(2,1)} %reshape.61), calls=%async_computation.1 | async-start | bytes 1048576 | tf_op jit(solution)/shard_map/all_to_all | solution.py:140
  123.5 0.2 reduce_sum.29
  123.7 0.6 divide_subtract_fusion
  124.3 18.6 %all-to-all-done.1 = bf16[128,2,960]{2,1,0:T(2,128)(2,1)S(1)} async-done(((bf16[128,2,960]{2,1,0:T(2,128)(2,1)}), bf16[128,2,960]{2,1,0:T(2,128)(2,1)S(1)}, u32[]{:S(2)}, u32[]{:S(2)}) %all-to-all-start.1) | async-done | bytes 491552 | tf_op jit(solution)/shard_map/all_to_all | solution.py:140
  143.0 0.8 reshape.62
  143.7 0.7 copy.37
  144.5 0.3 convolution_convert_fusion.1
  144.9 0.2 mul.156
  145.0 0.2 fusion.26
  145.2 0.7 copy.40
  145.9 0.2 mul.160
  146.1 0.2 fusion.29
  146.3 0.7 copy.41
  (20 shorter events, 0.1 us)
Async XLA Ops:
  10.2 21.4 %copy-start.5 = (s32[2,32]{1,0:T(2,128)S(1)}, s32[2,32]{1,0:T(2,128)}, u32[]{:S(2)}) copy-start(s32[2,32]{1,0:T(2,128)} %param.17) | copy-start | bytes 772
  13.1 37.8 %all-to-all-start = ((bf16[128,2,960]{2,1,0:T(2,128)(2,1)}), bf16[128,2,960]{2,1,0:T(2,128)(2,1)S(1)}, u32[]{:S(2)}, u32[]{:S(2)}) async-start(bf16[128,2,960]{2,1,0:T(2,128)(2,1)} %reshape.59), calls=%async_computation | async-start | bytes 1048576 | tf_op jit(solution)/shard_map/all_to_all | solution.py:123
  31.5 55.3 %all-gather.2.cloned.1.call-start = ((), (), s32[]{:S(2)}) async-start(), calls=%async_computation.3 | async-start | bytes 2457600 | tf_op jit(solution)/shard_map/all_gather | solution.py:95
  52.1 1.2 copy-start.1
  53.3 5.4 %copy-start.2 = (f32[1,43008]{1,0:T(1,128)S(1)}, f32[1,43008]{1,0:T(1,128)}, u32[]{:S(2)}) copy-start(f32[1,43008]{1,0:T(1,128)} %param.18) | copy-start | bytes 516100
  60.8 48.3 %all-to-all-start.2 = ((f32[128,1,336]{2,1,0:T(1,128)}), f32[128,1,336]{2,1,0:T(1,128)S(1)}, u32[]{:S(2)}, u32[]{:S(2)}) async-start(f32[128,1,336]{2,1,0:T(1,128)} %all_to_all.20), calls=%async_computation.2 | async-start | bytes 393216 | tf_op jit(solution)/shard_map/all_to_all | solution.py:152
  86.8 4.0 %copy-start = (bf16[1280,768]{0,1:T(8,128)(2,1)S(1)}, bf16[1280,768]{0,1:T(8,128)(2,1)}, u32[]{:S(2)}) copy-start(bf16[1280,768]{0,1:T(8,128)(2,1)} %all-gather.2.cloned.1.call-done) | copy-start | bytes 5898244
  107.2 16.5 %copy-start.6 = (f32[336]{0:T(512)S(1)}, f32[336]{0:T(512)}, u32[]{:S(2)}) copy-start(f32[336]{0:T(512)} %param.19) | copy-start | bytes 4036
  107.2 16.5 %copy-start.7 = (f32[336]{0:T(512)S(1)}, f32[336]{0:T(512)}, u32[]{:S(2)}) copy-start(f32[336]{0:T(512)} %param.20) | copy-start | bytes 4036
  107.2 16.5 %copy-start.8 = (f32[336]{0:T(512)S(1)}, f32[336]{0:T(512)}, u32[]{:S(2)}) copy-start(f32[336]{0:T(512)} %param.21) | copy-start | bytes 4036
  109.1 33.9 %all-to-all-start.1 = ((bf16[128,2,960]{2,1,0:T(2,128)(2,1)}), bf16[128,2,960]{2,1,0:T(2,128)(2,1)S(1)}, u32[]{:S(2)}, u32[]{:S(2)}) async-start(bf16[128,2,960]{2,1,0:T(2,128)(2,1)} %reshape.61), calls=%async_computation.1 | async-start | bytes 1048576 | tf_op jit(solution)/shard_map/all_to_all | solution.py:140
  143.7 1.3 copy-start.3
  144.8 1.3 copy-start.4
Sparse Core Ops, SparseCore 0:
  58.3 28.4 all-gather.1
where the time goes:
time: 154 us
  waiting for transfers between devices  53.9 us (35%)
  starting transfers between devices  40.2 us (26%)
  matrix products  18.2 us (12%)
  between operations  15.7 us (10%)
  local copies, waits for them, and re-layouts  13.7 us (9%)
  other arithmetic  12.2 us (8%)
    all_to_all x1, waiting for transfers between devices, per_device(): lax.all_to_all(route_rows(joint_map, joint_pieces), 'shard', split_axis=0...  18.7 us
    all_to_all x1, waiting for transfers between devices, per_device(): lax.all_to_all(own_result.reshape(shards, rows_dev, block_width), 'shard'...  18.6 us
    all_to_all x1, starting transfers between devices, per_device(): lax.all_to_all(route_rows(joint_map, joint_pieces), 'shard', split_axis=0...  18.4 us
    all_gather x1, waiting for transfers between devices, gather_columns(): return lax.all_gather(column_part, 'tensor', axis=1, tiled=True)  16.5 us
    all_to_all x1, starting transfers between devices, per_device(): lax.all_to_all(own_result.reshape(shards, rows_dev, block_width), 'shard'...  14.5 us
    dot_general x4, matrix products, newton_step(): lax.dot_general(full_iterate, polynomial, (((1,), (1,)), ((), ())), prefe...  10.4 us
    unnamed x25, local copies, waits for them, and re-layouts  7.42 us
    all_to_all x1, starting transfers between devices, per_device(): lax.all_to_all(vec_pieces, 'shard', split_axis=0, concat_axis=0, tiled=True)  7.25 us
  transfers between devices with their start and end apart: 4, of which 3 were waited for; matrix products, arithmetic and copies ran while one was open for 17% of the time, Pallas kernels for 0%

commit v1 on v0

--- a/solution.py
+++ b/solution.py
@@ -92,7 +92,9 @@
 
 
 def gather_columns(column_part):
-    return lax.all_gather(column_part, "tensor", axis=1, tiled=True)
+    return jnp.concatenate(
+        lax.all_to_all(jnp.stack([column_part] * lax.axis_size("tensor")), "tensor", 0, 0), axis=1
+    )
 
 
 def gather_gram(gram_part):

time: 154 us -> 150 us (0.974)
  between operations: 15.7 us -> 2.33 us
  starting transfers between devices: 40.2 us -> 45.5 us
  local copies, waits for them, and re-layouts: 13.7 us -> 17.8 us
    all_to_all x0 -> x1, waiting for transfers between devices: none -> 17.9 us  [gather_columns(): lax.all_to_all(jnp.stack([column_part] * lax.axis_size('tensor')), 'tenso...]
    all_gather x1 -> x0, waiting for transfers between devices: 16.5 us -> none  [gather_columns(): return lax.all_gather(column_part, 'tensor', axis=1, tiled=True)]
    all_to_all x0 -> x1, starting transfers between devices: none -> 4.14 us  [gather_columns(): lax.all_to_all(jnp.stack([column_part] * lax.axis_size('tensor')), 'tenso...]
    unnamed x25 -> x27, local copies, waits for them, and re-layouts: 7.42 us -> 10 us
    all_to_all x1, starting transfers between devices: 7.25 us -> 9.19 us  [per_device(): lax.all_to_all(vec_pieces, 'shard', split_axis=0, concat_axis=0, tiled=True)]
    reduce_sum x1, other arithmetic: 3.3 us -> 1.61 us  [normalized(): squares = jnp.sum(values * values)]
  transfers between devices with their start and end apart: 4 -> 4, of which waited for: 3 -> 3; matrix products, arithmetic and copies ran while one was open for 17% -> 16% of each run, Pallas kernels for 0% -> 0%
where the time goes in v1:
time: 150 us; the launch traced here: 149 us
  waiting for transfers between devices  55.2 us (37%)
  starting transfers between devices  45.5 us (30%)
  local copies, waits for them, and re-layouts  17.8 us (12%)
  matrix products  17.3 us (12%)
  other arithmetic  10.8 us (7%)
  between operations  2.33 us (2%)
    all_to_all x1, waiting for transfers between devices, per_device(): lax.all_to_all(route_rows(joint_map, joint_pieces), 'shard', split_axis=0...  18.8 us
    all_to_all x1, waiting for transfers between devices, per_device(): lax.all_to_all(own_result.reshape(shards, rows_dev, block_width), 'shard'...  18.6 us
    all_to_all x1, starting transfers between devices, per_device(): lax.all_to_all(route_rows(joint_map, joint_pieces), 'shard', split_axis=0...  18.4 us
    all_to_all x1, waiting for transfers between devices, gather_columns(): lax.all_to_all(jnp.stack([column_part] * lax.axis_size('tensor')), 'tenso...  17.9 us
    all_to_all x1, starting transfers between devices, per_device(): lax.all_to_all(own_result.reshape(shards, rows_dev, block_width), 'shard'...  13.7 us
    dot_general x4, matrix products, newton_step(): lax.dot_general(full_iterate, polynomial, (((1,), (1,)), ((), ())), prefe...  10.6 us
    unnamed x27, local copies, waits for them, and re-layouts  10 us
    all_to_all x1, starting transfers between devices, per_device(): lax.all_to_all(vec_pieces, 'shard', split_axis=0, concat_axis=0, tiled=True)  9.19 us
  transfers between devices with their start and end apart: 4, of which 3 were waited for; matrix products, arithmetic and copies ran while one was open for 16% of the time, Pallas kernels for 0%

profile of v1, /device:TPU:1, one launch (start us, length us, event | category | flops | bytes accessed | tf_op | source)
XLA Modules:
  0.0 149.0 jit_solution(17222949145101005453)
XLA Ops:
  0.6 0.8 slice_bitcast_fusion.1
  1.4 1.0 pad_maximum_fusion
  2.4 0.2 copy.32
  2.6 0.4 reshape.55
  3.1 0.3 convolution_convert_fusion
  3.4 0.3 copy.33
  3.7 1.4 copy.34
  5.1 1.6 %reshape.69 = bf16[128,2,960]{2,1,0:T(2,128)(2,1)} reshape(bf16[128,10,192]{2,1,0:T(8,128)(2,1)S(1)} %copy.34) | data formatting | bytes 983040
  6.6 18.4 %all-to-all-start = ((bf16[128,2,960]{2,1,0:T(2,128)(2,1)}), bf16[128,2,960]{2,1,0:T(2,128)(2,1)S(1)}, u32[]{:S(2)}, u32[]{:S(2)}) async-start(bf16[128,2,960]{2,1,0:T(2,128)(2,1)} %reshape.69), calls=%async_computation | async-start | bytes 1048576 | tf_op jit(solution)/shard_map/all_to_all | solution.py:125
  25.1 0.6 compare_reduce_fusion.1
  25.7 18.8 %all-to-all-done = bf16[128,2,960]{2,1,0:T(2,128)(2,1)S(1)} async-done(((bf16[128,2,960]{2,1,0:T(2,128)(2,1)}), bf16[128,2,960]{2,1,0:T(2,128)(2,1)S(1)}, u32[]{:S(2)}, u32[]{:S(2)}) %all-to-all-start) | async-done | bytes 491552 | tf_op jit(solution)/shard_map/all_to_all | solution.py:125
  44.5 0.8 reshape.70
  45.2 0.4 reshape.59
  45.6 0.4 copy.35
  46.0 0.8 copy-done.1
  46.8 4.8 %fusion.17 = (f32[1,192,1280]{2,1,0:T(8,128)}, bf16[1280,192]{0,1:T(8,128)(2,1)S(1)}, f32[1,192,1280]{2,1,0:T(8,128)}, f32[]{:T(128)}, bf16[192,1280]{1,0:T(8,128)(2,1)S(1)}) fusion(f32[1,192,1280]{2,1,0:T(8,128)S(1)} %copy-done.1, f32[1280,192]{0,1:T(8,128)S(1)} %copy.35, pred[]{:T(512)} %get-tuple-element.21, f32[1,192,1280]{2,1,0:T(8,128)} %param.16, ...), kind=kLoop, calls=%fused_computation.39 | loop fusion | flops 4177919 | bytes 5898246 | tf_op jit(solution)/shard_map/broadcast_in_dim | solution.py:163
  51.7 1.4 stack.2
  53.1 4.1 %all-to-all-start.1 = ((bf16[4,1280,192]{1,2,0:T(8,128)(2,1)}), bf16[4,1280,192]{1,2,0:T(8,128)(2,1)S(1)}, u32[]{:S(2)}, u32[]{:S(2)}) async-start(bf16[4,1280,192]{1,2,0:T(8,128)(2,1)} %stack.2), calls=%async_computation.1 | async-start | bytes 3932160 | tf_op jit(solution)/shard_map/all_to_all | solution.py:96
  57.2 0.5 broadcast.81
  57.7 1.0 reduce.7
  58.8 1.0 all_to_all.24
  60.5 0.3 convolution_convert_fusion.5
  60.8 0.4 fusion.3
  61.3 0.3 convolution_convert_fusion.4
  61.6 0.4 fusion.4
  62.0 17.9 %all-to-all-done.1 = bf16[4,1280,192]{1,2,0:T(8,128)(2,1)S(1)} async-done(((bf16[4,1280,192]{1,2,0:T(8,128)(2,1)}), bf16[4,1280,192]{1,2,0:T(8,128)(2,1)S(1)}, u32[]{:S(2)}, u32[]{:S(2)}) %all-to-all-start.1) | async-done | bytes 1966112 | tf_op jit(solution)/shard_map/all_to_all | solution.py:96
  79.9 9.2 %all-to-all-start.3 = ((f32[128,1,336]{2,1,0:T(1,128)}), f32[128,1,336]{2,1,0:T(1,128)S(1)}, u32[]{:S(2)}, u32[]{:S(2)}) async-start(f32[128,1,336]{2,1,0:T(1,128)} %all_to_all.24), calls=%async_computation.3 | async-start | bytes 393216 | tf_op jit(solution)/shard_map/all_to_all | solution.py:154
  89.1 1.6 %fusion = f32[]{:T(128)} fusion(bf16[4,1280,192]{1,2,0:T(8,128)(2,1)S(1)} %all-to-all-done.1), kind=kLoop, calls=%fused_computation.2 | loop fusion | flops 2949119 | bytes 1966084 | tf_op jit(solution)/shard_map/reduce_sum | solution.py:53
  91.4 0.4 fusion.1
  91.8 1.3 copy-done
  93.1 2.8 %convolution_convert_fusion.3 = bf16[768,768]{1,0:T(8,128)(2,1)} fusion(bf16[1280,768]{0,1:T(8,128)(2,1)S(1)} %bitcast.89), kind=kOutput, calls=%fused_computation.16 | convolution fusion | flops 1510539264 | bytes 3145728 | tf_op jit(solution)/shard_map/dot_general | solution.py:58
  95.8 6.0 %add_convert_fusion = bf16[1280,768]{0,1:T(8,128)(2,1)S(1)} fusion(bf16[1280,768]{0,1:T(8,128)(2,1)} %bitcast.90, bf16[768,768]{1,0:T(8,128)(2,1)} %convolution_convert_fusion.3), kind=kOutput, calls=%fused_computation.4 | convolution fusion | flops 2422800384 | bytes 5111808 | tf_op jit(solution)/shard_map/dot_general | solution.py:72
  101.8 1.3 copy-done.9
  103.1 2.8 %convolution_convert_fusion.2 = bf16[768,768]{1,0:T(8,128)(2,1)} fusion(bf16[1280,768]{0,1:T(8,128)(2,1)S(1)} %add_convert_fusion), kind=kOutput, calls=%fused_computation.15 | convolution fusion | flops 1510539264 | bytes 3145728 | tf_op jit(solution)/shard_map/dot_general | solution.py:58
  105.9 3.7 %fusion.5 = bf16[1280,192]{0,1:T(8,128)(2,1)S(1)} fusion(bf16[1280,192]{0,1:T(8,128)(2,1)S(1)} %fusion.4, bf16[1280,768]{0,1:T(8,128)(2,1)} %copy-done.9, bf16[768,768]{1,0:T(8,128)(2,1)} %convolution_convert_fusion.2, s32[]{:T(128)S(6)} %select_n.39, pred[]{:T(512)} %get-tuple-element.21), kind=kOutput, calls=%fused_computation.11 | convolution fusion | flops 605945856 | bytes 5212160 | tf_op jit(solution)/shard_map/dot_general | solution.py:72
  109.6 0.2 copy.36
  109.9 0.3 reshape.57
  110.2 1.6 %reshape.71 = bf16[128,2,960]{2,1,0:T(2,128)(2,1)} reshape(bf16[128,10,192]{2,1,0:T(8,128)(2,1)S(1)} %reshape.57) | data formatting | bytes 983040
  111.7 13.7 %all-to-all-start.2 = ((bf16[128,2,960]{2,1,0:T(2,128)(2,1)}), bf16[128,2,960]{2,1,0:T(2,128)(2,1)S(1)}, u32[]{:S(2)}, u32[]{:S(2)}) async-start(bf16[128,2,960]{2,1,0:T(2,128)(2,1)} %reshape.71), calls=%async_computation.2 | async-start | bytes 1048576 | tf_op jit(solution)/shard_map/all_to_all | solution.py:142
  125.5 0.2 reduce_sum.29
  125.7 0.6 divide_subtract_fusion
  126.3 18.6 %all-to-all-done.2 = bf16[128,2,960]{2,1,0:T(2,128)(2,1)S(1)} async-done(((bf16[128,2,960]{2,1,0:T(2,128)(2,1)}), bf16[128,2,960]{2,1,0:T(2,128)(2,1)S(1)}, u32[]{:S(2)}, u32[]{:S(2)}) %all-to-all-start.2) | async-done | bytes 491552 | tf_op jit(solution)/shard_map/all_to_all | solution.py:142
  144.9 0.8 reshape.72
  145.7 0.7 copy.37
  146.4 0.3 convolution_convert_fusion.1
  147.0 0.2 fusion.26
  147.2 0.7 copy.40
  148.2 0.7 copy.41
  (23 shorter events, 0.7 us)
Async XLA Ops:
  3.7 21.4 %copy-start.5 = (s32[2,32]{1,0:T(2,128)S(1)}, s32[2,32]{1,0:T(2,128)}, u32[]{:S(2)}) copy-start(s32[2,32]{1,0:T(2,128)} %param.17) | copy-start | bytes 772
  6.6 37.8 %all-to-all-start = ((bf16[128,2,960]{2,1,0:T(2,128)(2,1)}), bf16[128,2,960]{2,1,0:T(2,128)(2,1)S(1)}, u32[]{:S(2)}, u32[]{:S(2)}) async-start(bf16[128,2,960]{2,1,0:T(2,128)(2,1)} %reshape.69), calls=%async_computation | async-start | bytes 1048576 | tf_op jit(solution)/shard_map/all_to_all | solution.py:125
  45.6 1.2 copy-start.1
  53.1 4.7 %copy-start.2 = (f32[1,43008]{1,0:T(1,128)S(1)}, f32[1,43008]{1,0:T(1,128)}, u32[]{:S(2)}) copy-start(f32[1,43008]{1,0:T(1,128)} %param.18) | copy-start | bytes 516100
  53.1 26.8 %all-to-all-start.1 = ((bf16[4,1280,192]{1,2,0:T(8,128)(2,1)}), bf16[4,1280,192]{1,2,0:T(8,128)(2,1)S(1)}, u32[]{:S(2)}, u32[]{:S(2)}) async-start(bf16[4,1280,192]{1,2,0:T(8,128)(2,1)} %stack.2), calls=%async_computation.1 | async-start | bytes 3932160 | tf_op jit(solution)/shard_map/all_to_all | solution.py:96
  79.9 31.8 %all-to-all-start.3 = ((f32[128,1,336]{2,1,0:T(1,128)}), f32[128,1,336]{2,1,0:T(1,128)S(1)}, u32[]{:S(2)}, u32[]{:S(2)}) async-start(f32[128,1,336]{2,1,0:T(1,128)} %all_to_all.24), calls=%async_computation.3 | async-start | bytes 393216 | tf_op jit(solution)/shard_map/all_to_all | solution.py:154
  91.8 1.3 copy-start
  101.8 1.3 copy-start.9
  109.9 15.8 %copy-start.6 = (f32[336]{0:T(512)S(1)}, f32[336]{0:T(512)}, u32[]{:S(2)}) copy-start(f32[336]{0:T(512)} %param.19) | copy-start | bytes 4036
  109.9 15.8 %copy-start.7 = (f32[336]{0:T(512)S(1)}, f32[336]{0:T(512)}, u32[]{:S(2)}) copy-start(f32[336]{0:T(512)} %param.20) | copy-start | bytes 4036
  109.9 15.8 %copy-start.8 = (f32[336]{0:T(512)S(1)}, f32[336]{0:T(512)}, u32[]{:S(2)}) copy-start(f32[336]{0:T(512)} %param.21) | copy-start | bytes 4036
  111.7 33.2 %all-to-all-start.2 = ((bf16[128,2,960]{2,1,0:T(2,128)(2,1)}), bf16[128,2,960]{2,1,0:T(2,128)(2,1)S(1)}, u32[]{:S(2)}, u32[]{:S(2)}) async-start(bf16[128,2,960]{2,1,0:T(2,128)(2,1)} %reshape.71), calls=%async_computation.2 | async-start | bytes 1048576 | tf_op jit(solution)/shard_map/all_to_all | solution.py:142
  145.6 1.3 copy-start.3
  146.7 1.3 copy-start.4
